TPU v7x, 512 devices: a whole 4x4x16 slice. The times are simulated.
512 devices in a mesh: req: 128 (over y, z, core), tp: 4 (over x).
Axes of the slice: x: 4, y: 4, z: 16, core: 2. Of those that a mesh axis runs over, the one named last changes fastest.
Arguments:
- tokens: bfloat16 [131072, 3584], P('req', 'tp'), may hold values from -6 to 6
- key_value_weight: bfloat16 [3584, 1024], P('tp'), may hold values from -0.09375 to 0.09375
- adapter_down_maps: bfloat16 [128, 16, 3584], P('req', None, 'tp'), may hold values from -0.09375 to 0.09375
- adapter_up_maps: bfloat16 [128, 16, 1024], P('req', None, 'tp'), may hold values from -1.5 to 1.5
- block_adapter_ids: int32 [1024], P('req'), may hold values from 0 to 127, never falling along the last dimension, each value on 1 to 32 neighbouring positions
- block_live_rows: int32 [1024], P('req'), may hold values from 32 to 128
- adapter_storage_slot: int32 [128], replicated, may hold values from 0 to 127, each once
Outputs:
- keys_values: bfloat16 [131072, 1024], P('req', 'tp')
Inputs may be any that keep to these rules, and one draw needn't show every extreme that they name: `block_adapter_ids`: block ids never fall from one block to the next, every adapter id names at least one block, and one adapter names 32 blocks. `adapter_storage_slot`: each storage slot belongs to exactly one adapter.
All inputs are finite; a program needn't handle non-finite values.
Results may differ from a plain program's by a relative error of at most 0.003.
Values may be sent and summed in bfloat16 or wider, within the bound.
No kernel may reach another device: no remote copies, remote signals or barrier semaphores. Data moves between devices by JAX's collectives and lax.ppermute only.
A program may use at most 64 MiB of HBM per device.

v0:
```python
import numpy as np
import jax
import jax.numpy as jnp
from jax import lax
from jax.experimental.layout import Layout, with_layout_constraint
from jax.sharding import Mesh
from jax.sharding import PartitionSpec as P

adapter_scale = 0.5
ROWS = ("y", "z", "c")


def pick_entries(table, wanted, own_row, own_column, per_row, per_column):
    row_of = wanted // per_row
    inside = wanted % per_row
    entries = table[(own_column - inside % per_column) % per_column, inside // per_column]
    keep = (row_of == own_row)[:, None, None]
    return jnp.where(keep, entries, jnp.zeros_like(entries))


def shards(
    tokens,
    key_value_weight,
    adapter_down_maps,
    adapter_up_maps,
    block_adapter_ids,
    block_live_rows,
    adapter_storage_slot,
):
    rows_dev, width_dev = tokens.shape
    blocks_dev = block_adapter_ids.shape[0]
    block_rows = rows_dev // blocks_dev
    rank = adapter_down_maps.shape[1]
    local_columns = adapter_up_maps.shape[2]
    tp_size = key_value_weight.shape[1] // local_columns
    y_size = lax.axis_size("y")
    per_column = lax.axis_size("c")
    per_row = lax.axis_size("z") * per_column
    slot_ids = adapter_storage_slot[block_adapter_ids]
    my_row = lax.axis_index("y")
    base_partial = jnp.dot(tokens, key_value_weight, preferred_element_type=jnp.float32)
    outgoing = base_partial.reshape(rows_dev, tp_size, local_columns).transpose(1, 0, 2)
    incoming = lax.all_to_all(outgoing, "tp", 0, 0, tiled=False)
    both_maps = jnp.concatenate([adapter_down_maps, adapter_up_maps], axis=2)
    both_maps, outgoing = lax.optimization_barrier((both_maps, outgoing))
    column = lax.all_gather(both_maps, "z", axis=0, tiled=True)
    c_size = lax.axis_size("c")
    row_table = jnp.stack(
        [column]
        + [
            lax.ppermute(column, "c", [(i, (i + shift) % c_size) for i in range(c_size)])
            for shift in range(1, c_size)
        ]
    )
    row_ids = lax.all_to_all(
        jnp.broadcast_to(slot_ids[None], (y_size, blocks_dev)), "y", 0, 0, tiled=False
    )
    row_table, incoming = lax.optimization_barrier((row_table, incoming))
    base_result = with_layout_constraint(jnp.sum(incoming, axis=0), Layout((0, 1)))
    sent = pick_entries(
        row_table, row_ids.reshape(-1), my_row, lax.axis_index("c"), per_row, per_column
    )
    received = lax.all_to_all(
        sent.reshape((y_size, blocks_dev) + sent.shape[1:]), "y", 0, 0, tiled=False
    )
    received, base_result = lax.optimization_barrier((received, base_result))
    chosen_maps = jnp.sum(received, axis=0, dtype=received.dtype)
    chosen_down_maps = chosen_maps[:, :, :width_dev]
    chosen_up_maps = chosen_maps[:, :, width_dev:]
    blocked_input = tokens.reshape(blocks_dev, block_rows, width_dev)
    shrunk_partial = jnp.einsum(
        "qzo,qjo->qzj", blocked_input, chosen_down_maps, preferred_element_type=jnp.float32
    ).reshape(rows_dev, rank)
    shrunk = jnp.sum(
        lax.all_to_all(
            jnp.broadcast_to(shrunk_partial[None], (tp_size,) + shrunk_partial.shape),
            "tp",
            0,
            0,
            tiled=False,
        ),
        axis=0,
    )
    low_values = shrunk.astype(jnp.bfloat16)
    adapter_result = jnp.einsum(
        "bkr,brc->bkc",
        low_values.reshape(blocks_dev, block_rows, rank),
        chosen_up_maps,
        preferred_element_type=jnp.float32,
    ).reshape(rows_dev, local_columns)
    live_rows = (
        jnp.arange(block_rows, dtype=jnp.int32)[None, :] < block_live_rows[:, None]
    ).reshape(rows_dev, 1)
    adapted_output = base_result + adapter_scale * adapter_result
    return jnp.where(live_rows, adapted_output, jnp.zeros_like(adapted_output)).astype(jnp.bfloat16)


def split_mesh(mesh):
    devices = np.asarray(mesh.devices)
    first = devices[:, 0]
    y_size = len({d.coords[1] for d in first})
    z_size = len({d.coords[2] for d in first})
    c_size = len({d.core_on_chip for d in first})
    split = devices.reshape(y_size, z_size, c_size, devices.shape[1])
    for (yi, zi, ci), d in np.ndenumerate(split[:, :, :, 0]):
        assert (d.coords[1], d.coords[2], d.core_on_chip) == (
            sorted({e.coords[1] for e in first})[yi],
            sorted({e.coords[2] for e in first})[zi],
            sorted({e.core_on_chip for e in first})[ci],
        )
    return Mesh(split, ROWS + ("tp",))


def solution(mesh):
    in_specs = (
        P(ROWS, "tp"),
        P("tp", None),
        P(ROWS, None, "tp"),
        P(ROWS, None, "tp"),
        P(ROWS),
        P(ROWS),
        P(),
    )
    out_specs = P(ROWS, "tp")
    return jax.shard_map(
        shards, mesh=split_mesh(mesh), in_specs=in_specs, out_specs=out_specs, check_vma=False
    )
```

profile of v0, /device:TPU:416, one launch (start us, length us, event | category | flops | bytes accessed | tf_op | source)
XLA Modules:
  0.0 102.7 jit_solution(1394720287949011068)
XLA Ops:
  0.0 0.0 copy-start
  0.0 0.8 compare_select_fusion.2
  0.8 1.3 %gather_fusion = s32[8]{0:T(128)S(1)} fusion(s32[128]{0:T(128)} %param.13, s32[1024]{0:T(1024)S(1)} %pad_clamp_fusion), kind=kCustom, calls=%fused_computation | custom fusion | bytes 96 | tf_op jit(solution)/shard_map/gather | solution.py:39
  2.1 0.6 broadcast_in_dim.45
  2.7 4.5 %all-to-all-start = ((s32[4,1,8]{2,1,0:T(1,128)}), s32[4,1,8]{2,1,0:T(1,128)S(1)}, u32[]{:S(2)}, u32[]{:S(2)}) async-start(s32[4,1,8]{2,1,0:T(1,128)} %broadcast_in_dim.45), calls=%async_computation | async-start | bytes 4096 | tf_op jit(solution)/shard_map/all_to_all | solution.py:55
  7.2 0.0 copy-done
  7.2 5.9 %fusion.19 = f32[1024,1024]{0,1:T(8,128)} fusion(bf16[1024,896]{1,0:T(8,128)(2,1)S(1)} %copy-done, bf16[896,1024]{1,0:T(8,128)(2,1)} %param.8), kind=kOutput, calls=%fused_computation.50 | convolution fusion | flops 1879048192 | bytes 7864320 | tf_op jit(solution)/shard_map/dot_general | solution.py:41
  13.0 0.0 all-to-all-done
  13.0 0.0 copy-start.2
  13.0 0.0 copy-start.3
  13.0 5.0 %all-to-all-start.1 = ((f32[4,1024,256]{1,2,0:T(8,128)}), f32[4,1024,256]{1,2,0:T(8,128)}, u32[]{:S(2)}, u32[]{:S(2)}) async-start(f32[4,1024,256]{1,2,0:T(8,128)} %bitcast.38), calls=%async_computation.1 | async-start | bytes 8388608 | tf_op jit(solution)/shard_map/all_to_all | solution.py:43
  18.0 0.0 copy-done.2
  18.0 0.0 copy-done.3
  18.0 30.4 %all_gather.3 = bf16[16,16,1152]{2,1,0:T(8,128)(2,1)S(1)} all-gather(bf16[1,16,1152]{2,1,0:T(8,128)(2,1)S(1)} %pad_maximum_fusion.1), channel_id=1, replica_groups=mesh['y'=4,'z'=16,'c'=2,'tp'=4] {'z'}, dimensions={0}, use_global_device_ids=true | all-gather | bytes 626688 | tf_op jit(solution)/shard_map/all_gather | solution.py:46
  48.5 1.9 %collective-permute-start = (bf16[16,16,1152]{2,1,0:T(8,128)(2,1)S(1)}, bf16[16,16,1152]{2,1,0:T(8,128)(2,1)S(1)}, u32[]{:S(2)}, u32[]{:S(2)}) collective-permute-start(bf16[16,16,1152]{2,1,0:T(8,128)(2,1)S(1)} %all_gather.3), channel_id=1, source_target_pairs={{0,4},{4,0},{1,5},{5,1},{2,6},{6,2},{3,7},{7,3},{8,12},{12,8},{9,1... | collective-permute-start | bytes 1769480 | tf_op jit(solution)/shard_map/ppermute | solution.py:51
  50.4 0.5 broadcast.294
  50.9 0.7 reduce.3
  51.6 0.1 reshape.258
  51.7 0.6 collective-permute-done
  52.4 1.2 %pad_maximum_fusion = bf16[2,16,16,1152]{3,2,1,0:T(8,128)(2,1)} fusion(bf16[1,16,16,1152]{3,2,1,0:T(8,128)(2,1)S(1)} %bitcast.40, bf16[1,16,16,1152]{3,2,1,0:T(8,128)(2,1)S(1)} %bitcast.39), kind=kLoop, calls=%fused_computation.3 | loop fusion | flops 589824 | bytes 2359296 | tf_op jit(solution)/shard_map/stack | solution.py:48
  53.6 13.3 %all-to-all-done.1 = f32[4,1024,256]{1,2,0:T(8,128)} async-done(((f32[4,1024,256]{1,2,0:T(8,128)}), f32[4,1024,256]{1,2,0:T(8,128)}, u32[]{:S(2)}, u32[]{:S(2)}) %all-to-all-start.1) | async-done | bytes 4194336 | tf_op jit(solution)/shard_map/all_to_all | solution.py:43
  66.9 2.0 %gather_fusion.1 = bf16[32,16,1152]{2,1,0:T(8,128)(2,1)S(1)} fusion(bf16[2,16,16,1152]{3,2,1,0:T(8,128)(2,1)} %pad_maximum_fusion, s32[32]{0:T(128)S(1)} %fusion.18), kind=kCustom, calls=%fused_computation.1 | custom fusion | bytes 2359552 | tf_op jit(solution)/shard_map/gather | solution.py:16
  68.9 1.2 %broadcast_select_fusion = bf16[4,8,16,1152]{3,2,1,0:T(8,128)(2,1)} fusion(bf16[4,8,16,1152]{3,2,1,0:T(8,128)(2,1)S(1)} %bitcast.37, pred[4,8]{1,0:T(4,128)(4,1)S(1)} %fusion.8), kind=kLoop, calls=%fused_computation.4 | loop fusion | flops 589824 | bytes 2359328 | tf_op jit(solution)/shard_map/jit(_where)/select_n | solution.py:18
  70.1 4.5 %all-to-all-start.2 = ((bf16[4,8,16,1152]{3,2,1,0:T(8,128)(2,1)}), bf16[4,8,16,1152]{3,2,1,0:T(8,128)(2,1)S(1)}, u32[]{:S(2)}, u32[]{:S(2)}) async-start(bf16[4,8,16,1152]{3,2,1,0:T(8,128)(2,1)} %broadcast_select_fusion), calls=%async_computation.2 | async-start | bytes 2359296 | tf_op jit(solution)/shard_map/all_to_all | solution.py:63
  74.6 3.7 %reduce_sum.27 = f32[1024,256]{0,1:T(8,128)} reduce(f32[4,1024,256]{1,2,0:T(8,128)} %all-to-all-done.1, f32[]{:T(128)} %constant.75.clone.1), dimensions={0}, to_apply=%region_0.0 | reduce | flops 786432 | bytes 5242884 | tf_op jit(solution)/shard_map/reduce_sum | solution.py:59
  78.3 2.5 %copy.11 = f32[1024,256]{1,0:T(8,128)} copy(f32[1024,256]{0,1:T(8,128)} %reduce_sum.27) | data formatting | bytes 2097152 | tf_op jit(solution)/shard_map/reduce_sum | solution.py:59
  80.8 8.8 %all-to-all-done.2 = bf16[4,8,16,1152]{3,2,1,0:T(8,128)(2,1)S(1)} async-done(((bf16[4,8,16,1152]{3,2,1,0:T(8,128)(2,1)}), bf16[4,8,16,1152]{3,2,1,0:T(8,128)(2,1)S(1)}, u32[]{:S(2)}, u32[]{:S(2)}) %all-to-all-start.2) | async-done | bytes 1179680 | tf_op jit(solution)/shard_map/all_to_all | solution.py:63
  89.7 0.2 reduce_sum.28
  89.9 0.0 copy-start.4
  89.9 0.0 copy-start.1
  89.9 0.6 convolution_bitcast_fusion
  90.5 0.7 broadcast_in_dim.49
  91.3 3.4 %all-to-all-start.3 = ((f32[4,1024,16]{1,2,0:T(8,128)}), f32[4,1024,16]{1,2,0:T(8,128)S(1)}, u32[]{:S(2)}, u32[]{:S(2)}) async-start(f32[4,1024,16]{1,2,0:T(8,128)} %broadcast_in_dim.49), calls=%async_computation.3 | async-start | bytes 524288 | tf_op jit(solution)/shard_map/all_to_all | solution.py:75
  94.7 0.0 copy-done.4
  94.7 0.1 fusion.6
  94.8 6.6 %all-to-all-done.3 = f32[4,1024,16]{1,2,0:T(8,128)S(1)} async-done(((f32[4,1024,16]{1,2,0:T(8,128)}), f32[4,1024,16]{1,2,0:T(8,128)S(1)}, u32[]{:S(2)}, u32[]{:S(2)}) %all-to-all-start.3) | async-done | bytes 262176 | tf_op jit(solution)/shard_map/all_to_all | solution.py:75
  101.3 0.3 convolution_multiply_fusion
  101.7 0.0 copy-done.1
  101.7 1.0 %fusion.1 = bf16[1024,256]{1,0:T(8,128)(2,1)} fusion(f32[1024,256]{1,0:T(8,128)S(1)} %copy-done.1, f32[8,128,256]{2,1,0:T(8,128)S(1)} %convolution_multiply_fusion, pred[1024]{0:T(1024)(128)(4,1)S(1)} %fusion.6), kind=kLoop, calls=%fused_computation.8 | loop fusion | flops 786432 | bytes 2622464 | tf_op jit(solution)/shard_map/convert_element_type | solution.py:95
  (6 shorter events, 0.1 us)
Async XLA Ops:
  0.0 7.2 %copy-start = (bf16[1024,896]{1,0:T(8,128)(2,1)S(1)}, bf16[1024,896]{1,0:T(8,128)(2,1)}, u32[]{:S(2)}) copy-start(bf16[1024,896]{1,0:T(8,128)(2,1)} %param.7) | copy-start | bytes 5505028
  2.7 10.3 %all-to-all-start = ((s32[4,1,8]{2,1,0:T(1,128)}), s32[4,1,8]{2,1,0:T(1,128)S(1)}, u32[]{:S(2)}, u32[]{:S(2)}) async-start(s32[4,1,8]{2,1,0:T(1,128)} %broadcast_in_dim.45), calls=%async_computation | async-start | bytes 4096 | tf_op jit(solution)/shard_map/all_to_all | solution.py:55
  13.0 5.0 %copy-start.2 = (bf16[1,16,896]{2,1,0:T(8,128)(2,1)S(1)}, bf16[1,16,896]{2,1,0:T(8,128)(2,1)}, u32[]{:S(2)}) copy-start(bf16[1,16,896]{2,1,0:T(8,128)(2,1)} %param.9) | copy-start | bytes 86020
  13.0 5.0 %copy-start.3 = (bf16[1,16,256]{2,1,0:T(8,128)(2,1)S(1)}, bf16[1,16,256]{2,1,0:T(8,128)(2,1)}, u32[]{:S(2)}) copy-start(bf16[1,16,256]{2,1,0:T(8,128)(2,1)} %param.10) | copy-start | bytes 24580
  13.0 53.8 %all-to-all-start.1 = ((f32[4,1024,256]{1,2,0:T(8,128)}), f32[4,1024,256]{1,2,0:T(8,128)}, u32[]{:S(2)}, u32[]{:S(2)}) async-start(f32[4,1024,256]{1,2,0:T(8,128)} %bitcast.38), calls=%async_computation.1 | async-start | bytes 8388608 | tf_op jit(solution)/shard_map/all_to_all | solution.py:43
  48.5 3.9 %collective-permute-start = (bf16[16,16,1152]{2,1,0:T(8,128)(2,1)S(1)}, bf16[16,16,1152]{2,1,0:T(8,128)(2,1)S(1)}, u32[]{:S(2)}, u32[]{:S(2)}) collective-permute-start(bf16[16,16,1152]{2,1,0:T(8,128)(2,1)S(1)} %all_gather.3), channel_id=1, source_target_pairs={{0,4},{4,0},{1,5},{5,1},{2,6},{6,2},{3,7},{7,3},{8,12},{12,8},{9,1... | collective-permute-start | bytes 1769480 | tf_op jit(solution)/shard_map/ppermute | solution.py:51
  70.1 19.6 %all-to-all-start.2 = ((bf16[4,8,16,1152]{3,2,1,0:T(8,128)(2,1)}), bf16[4,8,16,1152]{3,2,1,0:T(8,128)(2,1)S(1)}, u32[]{:S(2)}, u32[]{:S(2)}) async-start(bf16[4,8,16,1152]{3,2,1,0:T(8,128)(2,1)} %broadcast_select_fusion), calls=%async_computation.2 | async-start | bytes 2359296 | tf_op jit(solution)/shard_map/all_to_all | solution.py:63
  89.9 4.8 %copy-start.4 = (s32[8]{0:T(128)S(1)}, s32[8]{0:T(128)}, u32[]{:S(2)}) copy-start(s32[8]{0:T(128)} %param.12) | copy-start | bytes 100
  89.9 11.8 %copy-start.1 = (f32[1024,256]{1,0:T(8,128)S(1)}, f32[1024,256]{1,0:T(8,128)}, u32[]{:S(2)}) copy-start(f32[1024,256]{1,0:T(8,128)} %copy.11) | copy-start | bytes 3145732
  91.3 10.1 %all-to-all-start.3 = ((f32[4,1024,16]{1,2,0:T(8,128)}), f32[4,1024,16]{1,2,0:T(8,128)S(1)}, u32[]{:S(2)}, u32[]{:S(2)}) async-start(f32[4,1024,16]{1,2,0:T(8,128)} %broadcast_in_dim.49), calls=%async_computation.3 | async-start | bytes 524288 | tf_op jit(solution)/shard_map/all_to_all | solution.py:75
where the time goes:
time: 103 us
  blocking collectives  30.4 us (30%)
  waiting for transfers between devices  29.3 us (28%)
  starting transfers between devices  19.3 us (19%)
  other arithmetic  8.97 us (9%)
  local copies, waits for them, and re-layouts  7.78 us (8%)
  matrix products  6.85 us (7%)
    all_gather x1, blocking collectives, shards(): column = lax.all_gather(both_maps, 'z', axis=0, tiled=True)  30.4 us
    all_to_all x1, waiting for transfers between devices, shards(): incoming = lax.all_to_all(outgoing, 'tp', 0, 0, tiled=False)  13.3 us
    all_to_all x1, waiting for transfers between devices, shards(): lax.all_to_all(sent.reshape((y_size, blocks_dev) + sent.shape[1:]), 'y',...  8.83 us
    all_to_all x1, waiting for transfers between devices, shards(): lax.all_to_all(jnp.broadcast_to(shrunk_partial[None], (tp_size,) + shrunk...  6.56 us
    dot_general x1, matrix products, shards(): jnp.dot(tokens, key_value_weight, preferred_element_type=jnp.float32)  5.86 us
    all_to_all x1, starting transfers between devices, shards(): incoming = lax.all_to_all(outgoing, 'tp', 0, 0, tiled=False)  4.98 us
    all_to_all x1, starting transfers between devices, shards(): lax.all_to_all(sent.reshape((y_size, blocks_dev) + sent.shape[1:]), 'y',...  4.52 us
    all_to_all x1, starting transfers between devices, shards(): lax.all_to_all(jnp.broadcast_to(slot_ids[None], (y_size, blocks_dev)), 'y...  4.46 us
  transfers between devices with their start and end apart: 5, of which 4 were waited for; matrix products, arithmetic and copies ran while one was open for 14% of the time, Pallas kernels for 0%

commit v1 on v0

--- a/solution.py
+++ b/solution.py
@@ -43,7 +43,10 @@
     incoming = lax.all_to_all(outgoing, "tp", 0, 0, tiled=False)
     both_maps = jnp.concatenate([adapter_down_maps, adapter_up_maps], axis=2)
     both_maps, outgoing = lax.optimization_barrier((both_maps, outgoing))
-    column = lax.all_gather(both_maps, "z", axis=0, tiled=True)
+    handle_the_desk = lambda buf: jnp.concatenate(
+        lax.all_to_all(jnp.stack(lax.axis_size("z") * [buf], 0), "z", 0, 0), axis=0
+    )
+    column = handle_the_desk(both_maps)
     c_size = lax.axis_size("c")
     row_table = jnp.stack(
         [column]

time: 103 us -> 151 us (1.47)
  the two profiles are of different devices: /device:TPU:416 before, /device:TPU:32 now
where the time goes in v1:
time: 151 us; the launch traced here: 150 us
  waiting for transfers between devices  57.2 us (38%)
  blocking collectives  49.2 us (33%)
  starting transfers between devices  19.2 us (13%)
  other arithmetic  9.75 us (6%)
  local copies, waits for them, and re-layouts  7.84 us (5%)
  matrix products  6.84 us (5%)
    all_to_all x1, blocking collectives, shards(): lax.all_to_all(jnp.stack(lax.axis_size('z') * [buf], 0), 'z', 0, 0)  49.2 us
    all_to_all x1, waiting for transfers between devices, shards(): incoming = lax.all_to_all(outgoing, 'tp', 0, 0, tiled=False)  42.3 us
    all_to_all x1, waiting for transfers between devices, shards(): lax.all_to_all(sent.reshape((y_size, blocks_dev) + sent.shape[1:]), 'y',...  7.71 us
    all_to_all x1, waiting for transfers between devices, shards(): lax.all_to_all(jnp.broadcast_to(shrunk_partial[None], (tp_size,) + shrunk...  6.56 us
    dot_general x1, matrix products, shards(): jnp.dot(tokens, key_value_weight, preferred_element_type=jnp.float32)  5.85 us
    all_to_all x1, starting transfers between devices, shards(): incoming = lax.all_to_all(outgoing, 'tp', 0, 0, tiled=False)  4.85 us
    all_to_all x1, starting transfers between devices, shards(): lax.all_to_all(sent.reshape((y_size, blocks_dev) + sent.shape[1:]), 'y',...  4.53 us
    all_to_all x1, starting transfers between devices, shards(): lax.all_to_all(jnp.broadcast_to(slot_ids[None], (y_size, blocks_dev)), 'y...  4.46 us
  transfers between devices with their start and end apart: 5, of which 4 were waited for; matrix products, arithmetic and copies ran while one was open for 10% of the time, Pallas kernels for 0%

profile of v1, /device:TPU:32, one launch (start us, length us, event | category | flops | bytes accessed | tf_op | source)
XLA Modules:
  0.0 150.1 jit_solution(6993332679952253321)
XLA Ops:
  0.0 0.0 copy-start
  0.0 0.8 compare_select_fusion.2
  0.8 1.3 gather_fusion
  2.1 0.6 broadcast_in_dim.45
  2.7 4.5 %all-to-all-start = ((s32[4,1,8]{2,1,0:T(1,128)}), s32[4,1,8]{2,1,0:T(1,128)S(1)}, u32[]{:S(2)}, u32[]{:S(2)}) async-start(s32[4,1,8]{2,1,0:T(1,128)} %broadcast_in_dim.45), calls=%async_computation | async-start | bytes 4096 | tf_op jit(solution)/shard_map/all_to_all | solution.py:58
  7.2 0.8 pad_maximum_fusion.1
  7.9 0.0 copy-done
  7.9 5.8 %fusion.19 = f32[1024,1024]{0,1:T(8,128)} fusion(bf16[1024,896]{1,0:T(8,128)(2,1)S(1)} %copy-done, bf16[896,1024]{1,0:T(8,128)(2,1)} %param.8), kind=kOutput, calls=%fused_computation.50 | convolution fusion | flops 1879048192 | bytes 7864320 | tf_op jit(solution)/shard_map/dot_general | solution.py:41
  13.8 0.0 all-to-all-done
  13.8 49.2 %all_to_all.26 = bf16[16,1,16,1152]{3,2,1,0:T(8,128)(2,1)S(1)} all-to-all(bf16[16,1,16,1152]{3,2,1,0:T(8,128)(2,1)S(1)} %stack.6), channel_id=1, replica_groups=mesh['y'=4,'z'=16,'c'=2,'tp'=4] {'z'}, dimensions={0} | all-to-all | bytes 1179648 | tf_op jit(solution)/shard_map/all_to_all | solution.py:47
  63.0 4.9 %all-to-all-start.2 = ((f32[4,1024,256]{1,2,0:T(8,128)}), f32[4,1024,256]{1,2,0:T(8,128)}, u32[]{:S(2)}, u32[]{:S(2)}) async-start(f32[4,1024,256]{1,2,0:T(8,128)} %bitcast.40), calls=%async_computation.2 | async-start | bytes 8388608 | tf_op jit(solution)/shard_map/all_to_all | solution.py:43
  67.9 1.9 %collective-permute-start = (bf16[16,16,1152]{2,1,0:T(8,128)(2,1)S(1)}, bf16[16,16,1152]{2,1,0:T(8,128)(2,1)S(1)}, u32[]{:S(2)}, u32[]{:S(2)}) collective-permute-start(bf16[16,16,1152]{2,1,0:T(8,128)(2,1)S(1)} %bitcast.41), channel_id=1, source_target_pairs={{0,4},{4,0},{1,5},{5,1},{2,6},{6,2},{3,7},{7,3},{8,12},{12,8},{9,1... | collective-permute-start | bytes 1769480 | tf_op jit(solution)/shard_map/ppermute | solution.py:54
  69.8 0.5 broadcast.297
  70.3 0.7 reduce.3
  71.0 0.1 reshape.265
  71.1 0.6 collective-permute-done
  71.8 1.2 pad_maximum_fusion
  73.0 42.3 %all-to-all-done.2 = f32[4,1024,256]{1,2,0:T(8,128)} async-done(((f32[4,1024,256]{1,2,0:T(8,128)}), f32[4,1024,256]{1,2,0:T(8,128)}, u32[]{:S(2)}, u32[]{:S(2)}) %all-to-all-start.2) | async-done | bytes 4194336 | tf_op jit(solution)/shard_map/all_to_all | solution.py:43
  115.4 2.0 %gather_fusion.1 = bf16[32,16,1152]{2,1,0:T(8,128)(2,1)S(1)} fusion(bf16[2,16,16,1152]{3,2,1,0:T(8,128)(2,1)} %pad_maximum_fusion, s32[32]{0:T(128)S(1)} %fusion.18), kind=kCustom, calls=%fused_computation.1 | custom fusion | bytes 2359552 | tf_op jit(solution)/shard_map/gather | solution.py:16
  117.4 1.2 broadcast_select_fusion
  118.6 4.5 %all-to-all-start.3 = ((bf16[4,8,16,1152]{3,2,1,0:T(8,128)(2,1)}), bf16[4,8,16,1152]{3,2,1,0:T(8,128)(2,1)S(1)}, u32[]{:S(2)}, u32[]{:S(2)}) async-start(bf16[4,8,16,1152]{3,2,1,0:T(8,128)(2,1)} %broadcast_select_fusion), calls=%async_computation.3 | async-start | bytes 2359296 | tf_op jit(solution)/shard_map/all_to_all | solution.py:66
  123.1 3.7 %reduce_sum.27 = f32[1024,256]{0,1:T(8,128)} reduce(f32[4,1024,256]{1,2,0:T(8,128)} %all-to-all-done.2, f32[]{:T(128)} %constant.75.clone.1), dimensions={0}, to_apply=%region_0.0 | reduce | flops 786432 | bytes 5242884 | tf_op jit(solution)/shard_map/reduce_sum | solution.py:62
  126.8 2.5 %copy.11 = f32[1024,256]{1,0:T(8,128)} copy(f32[1024,256]{0,1:T(8,128)} %reduce_sum.27) | data formatting | bytes 2097152 | tf_op jit(solution)/shard_map/reduce_sum | solution.py:62
  129.4 7.7 %all-to-all-done.3 = bf16[4,8,16,1152]{3,2,1,0:T(8,128)(2,1)S(1)} async-done(((bf16[4,8,16,1152]{3,2,1,0:T(8,128)(2,1)}), bf16[4,8,16,1152]{3,2,1,0:T(8,128)(2,1)S(1)}, u32[]{:S(2)}, u32[]{:S(2)}) %all-to-all-start.3) | async-done | bytes 1179680 | tf_op jit(solution)/shard_map/all_to_all | solution.py:66
  137.1 0.2 reduce_sum.28
  137.3 0.0 copy-start.2
  137.3 0.0 copy-start.1
  137.3 0.6 convolution_bitcast_fusion
  137.9 0.7 broadcast_in_dim.49
  138.7 3.4 %all-to-all-start.4 = ((f32[4,1024,16]{1,2,0:T(8,128)}), f32[4,1024,16]{1,2,0:T(8,128)S(1)}, u32[]{:S(2)}, u32[]{:S(2)}) async-start(f32[4,1024,16]{1,2,0:T(8,128)} %broadcast_in_dim.49), calls=%async_computation.4 | async-start | bytes 524288 | tf_op jit(solution)/shard_map/all_to_all | solution.py:78
  142.1 0.0 copy-done.2
  142.1 0.1 fusion.6
  142.2 6.6 %all-to-all-done.4 = f32[4,1024,16]{1,2,0:T(8,128)S(1)} async-done(((f32[4,1024,16]{1,2,0:T(8,128)}), f32[4,1024,16]{1,2,0:T(8,128)S(1)}, u32[]{:S(2)}, u32[]{:S(2)}) %all-to-all-start.4) | async-done | bytes 262176 | tf_op jit(solution)/shard_map/all_to_all | solution.py:78
  148.7 0.3 convolution_multiply_fusion
  149.1 0.0 copy-done.1
  149.1 1.0 fusion.1
  (6 shorter events, 0.1 us)
Async XLA Ops:
  0.0 7.9 %copy-start = (bf16[1024,896]{1,0:T(8,128)(2,1)S(1)}, bf16[1024,896]{1,0:T(8,128)(2,1)}, u32[]{:S(2)}) copy-start(bf16[1024,896]{1,0:T(8,128)(2,1)} %param.7) | copy-start | bytes 5505028
  2.7 11.1 %all-to-all-start = ((s32[4,1,8]{2,1,0:T(1,128)}), s32[4,1,8]{2,1,0:T(1,128)S(1)}, u32[]{:S(2)}, u32[]{:S(2)}) async-start(s32[4,1,8]{2,1,0:T(1,128)} %broadcast_in_dim.45), calls=%async_computation | async-start | bytes 4096 | tf_op jit(solution)/shard_map/all_to_all | solution.py:58
  63.0 52.3 %all-to-all-start.2 = ((f32[4,1024,256]{1,2,0:T(8,128)}), f32[4,1024,256]{1,2,0:T(8,128)}, u32[]{:S(2)}, u32[]{:S(2)}) async-start(f32[4,1024,256]{1,2,0:T(8,128)} %bitcast.40), calls=%async_computation.2 | async-start | bytes 8388608 | tf_op jit(solution)/shard_map/all_to_all | solution.py:43
  67.9 3.9 %collective-permute-start = (bf16[16,16,1152]{2,1,0:T(8,128)(2,1)S(1)}, bf16[16,16,1152]{2,1,0:T(8,128)(2,1)S(1)}, u32[]{:S(2)}, u32[]{:S(2)}) collective-permute-start(bf16[16,16,1152]{2,1,0:T(8,128)(2,1)S(1)} %bitcast.41), channel_id=1, source_target_pairs={{0,4},{4,0},{1,5},{5,1},{2,6},{6,2},{3,7},{7,3},{8,12},{12,8},{9,1... | collective-permute-start | bytes 1769480 | tf_op jit(solution)/shard_map/ppermute | solution.py:54
  118.6 18.5 %all-to-all-start.3 = ((bf16[4,8,16,1152]{3,2,1,0:T(8,128)(2,1)}), bf16[4,8,16,1152]{3,2,1,0:T(8,128)(2,1)S(1)}, u32[]{:S(2)}, u32[]{:S(2)}) async-start(bf16[4,8,16,1152]{3,2,1,0:T(8,128)(2,1)} %broadcast_select_fusion), calls=%async_computation.3 | async-start | bytes 2359296 | tf_op jit(solution)/shard_map/all_to_all | solution.py:66
  137.3 4.8 %copy-start.2 = (s32[8]{0:T(128)S(1)}, s32[8]{0:T(128)}, u32[]{:S(2)}) copy-start(s32[8]{0:T(128)} %param.12) | copy-start | bytes 100
  137.3 11.8 %copy-start.1 = (f32[1024,256]{1,0:T(8,128)S(1)}, f32[1024,256]{1,0:T(8,128)}, u32[]{:S(2)}) copy-start(f32[1024,256]{1,0:T(8,128)} %copy.11) | copy-start | bytes 3145732
  138.7 10.1 %all-to-all-start.4 = ((f32[4,1024,16]{1,2,0:T(8,128)}), f32[4,1024,16]{1,2,0:T(8,128)S(1)}, u32[]{:S(2)}, u32[]{:S(2)}) async-start(f32[4,1024,16]{1,2,0:T(8,128)} %broadcast_in_dim.49), calls=%async_computation.4 | async-start | bytes 524288 | tf_op jit(solution)/shard_map/all_to_all | solution.py:78
